TPU v7x, 256 devices: a whole 4x4x8 slice. The times are simulated.
256 devices in a mesh: sect: 2 (over y_lo), batch: 16 (over z, core), head: 8 (over x, y_hi).
Axes of the slice: x: 4, y: 4 (y_hi: 2, y_lo: 2; y = y_hi * 2 + y_lo), z: 8, core: 2. Of those that a mesh axis runs over, the one named last changes fastest.
Arguments:
- queries: bfloat16 [96, 16, 512], P('batch', 'head', 'sect'), may hold values from -51 to 51
- newest_key_value: bfloat16 [96, 4, 256], P('batch'), may hold values from -5 to 5
- page_cache: bfloat16 [96, 256, 64, 256], P('batch', ('sect', 'head')), may hold values from -4 to 4
- lengths: int32 [96], P('batch'), may hold values from 2048 to 4096, as said below
- page_ids: int32 [96, 4, 32], P('batch'), may hold values from 0 to 63, as said below
- out_weight: bfloat16 [8192, 4096], P(('sect', 'head'), 'batch'), may hold values from -0.0625 to 0.0625
- residual: bfloat16 [96, 4096], P(None, 'batch'), may hold values from -2 to 2
- norm_gain: float32 [4096], P('batch'), may hold values from 0.25 to 1.75
- expert_ids: int32 [96, 8], replicated, may hold values from 0 to 63, all different within a row; in each aligned block of 96 rows (0 to 95, 96 to 191, ...) at most 24 rows name the same one
- route_weight: float32 [96, 8], replicated, may hold values from 0.1 to 1
- gate_up_weight: bfloat16 [32, 4096, 2, 3072], P(('sect', 'batch'), None, None, 'head'), may hold values from -0.09375 to 0.09375
- down_weight: bfloat16 [32, 3072, 4096], P(('sect', 'batch'), 'head'), may hold values from -0.15625 to 0.15625
Outputs:
- layer_out: bfloat16 [96, 4096], P(None, 'batch')
Inputs may be any that keep to these rules, and one draw needn't show every extreme that they name: `lengths`: some sequence holds exactly 4096 cached tokens and some exactly 2048. `page_ids`: each row lists 32 different pages in ascending order, all below the number of pages that hold the sequence's cached tokens, and always the last of those pages. `expert_ids`: each row names 8 different experts; over all rows no expert is named by more than 24 rows, a bound that some block reaches.
All inputs are finite; a program needn't handle non-finite values.
Results may differ from a plain program's by a relative error of at most 0.025.
Values may be sent and summed in bfloat16 or wider, within the bound.
No kernel may reach another device: no remote copies, remote signals or barrier semaphores. Data moves between devices by JAX's collectives and lax.ppermute only.
A program may use at most 128 MiB of HBM per device.

v0:
```python
import math
import jax
import jax.numpy as jnp
from jax import lax
from jax.sharding import PartitionSpec as P

D = 4096
EXPERTS = 64
NEG_FILL = -1e30
NORM_EPS = 1e-06


def copy_for_each(shard, axis):
    copies = jnp.broadcast_to(shard, (lax.axis_size(axis), *shard.shape))
    return lax.all_to_all(copies, axis, split_axis=0, concat_axis=0, tiled=True)


def in_order(pieces, dim):
    lengths = list(pieces.shape[1:])
    lengths[dim] *= pieces.shape[0]
    return jnp.moveaxis(pieces, 0, dim).reshape(lengths)


def gathered_copies(shard, axis, dim):
    pieces = copy_for_each(shard, axis)
    return in_order(pieces, dim)


def from_partner(shard, axis, distance):
    return lax.ppermute(shard, axis, [(i, i ^ 1 << distance) for i in range(lax.axis_size(axis))])


def taken_together(shard, axis):
    return copy_for_each(shard, axis).astype(jnp.float32).sum(axis=0)


def of_everyone(shard, axis):
    return copy_for_each(shard, axis).sum(axis=0)


def merge_pair(first, second):
    first_max, first_sum, first_acc = first
    second_max, second_sum, second_acc = second
    joined = jnp.maximum(first_max, second_max)
    first_factor = jnp.exp(first_max - joined)
    second_factor = jnp.exp(second_max - joined)
    return (
        joined,
        first_sum * first_factor + second_sum * second_factor,
        first_acc * first_factor[..., None] + second_acc * second_factor[..., None],
    )


def head_slice(partial_value, begin_at, span_size):
    return tuple(
        (lax.dynamic_slice_in_dim(member, begin_at, span_size, 1) for member in partial_value)
    )


def on_device(
    queries,
    newest_key_value,
    page_cache,
    lengths,
    page_ids,
    out_weight,
    residual,
    norm_gain,
    expert_ids,
    route_weight,
    gate_up_weight,
    down_weight,
):
    seq_count = queries.shape[0]
    head_dim = newest_key_value.shape[2] // 2
    kv_heads = newest_key_value.shape[1]
    sect_size = lax.axis_size("sect")
    head_size = lax.axis_size("head")
    batch_size = lax.axis_size("batch")
    group_size = sect_size * head_size // kv_heads
    position = lax.axis_index("sect") * head_size + lax.axis_index("head")
    kv_index = position // group_size
    quarter = position % group_size
    local_pages = page_cache.shape[1]
    page_len = page_cache.shape[2]
    scaling = 1.0 / math.sqrt(head_dim)
    all_heads = lax.all_gather(queries, "head", axis=1, tiled=True)
    kv_local = kv_index % (kv_heads // sect_size)
    group_query = lax.dynamic_slice_in_dim(all_heads, kv_local * head_dim, head_dim, 2)
    heads_dev = all_heads.shape[1] // group_size
    block_cols = heads_dev * head_dim
    chosen = lax.dynamic_index_in_dim(page_ids, kv_index, 1, keepdims=False)
    leading_page = quarter * local_pages
    page_number = jnp.broadcast_to(
        leading_page + jnp.arange(local_pages, dtype=jnp.int32), (seq_count, local_pages)
    )
    page_used = jnp.any(chosen[:, :, None] == page_number[:, None, :], axis=1)
    token_place = (
        page_number[:, :, None] * page_len + jnp.arange(page_len, dtype=jnp.int32)[None, None, :]
    )
    key_count = page_cache.shape[1] * page_len
    usable_pages = (page_used[:, :, None] & (token_place < lengths[:, None, None])).reshape(
        seq_count, key_count
    )
    gathered_keys = page_cache[..., :head_dim].reshape(seq_count, key_count, head_dim)
    gathered_values = page_cache[..., head_dim:].reshape(seq_count, key_count, head_dim)
    scores = (
        jnp.einsum("shd,skd->shk", group_query, gathered_keys, preferred_element_type=jnp.float32)
        * scaling
    )
    scores = jnp.where(usable_pages[:, None, :], scores, NEG_FILL)
    newest_entry = lax.dynamic_index_in_dim(newest_key_value, kv_index, 1, keepdims=False)
    fresh_score = (
        jnp.einsum(
            "shd,sd->sh",
            group_query,
            newest_entry[:, :head_dim],
            preferred_element_type=jnp.float32,
        )
        * scaling
    )
    leading = quarter == 0
    fresh_score = jnp.where(leading, fresh_score, NEG_FILL)
    running_max = jnp.maximum(jnp.max(scores, axis=2), fresh_score)
    weights = jnp.where(usable_pages[:, None, :], jnp.exp(scores - running_max[..., None]), 0.0)
    fresh_weight = jnp.where(leading, jnp.exp(fresh_score - running_max), 0.0)
    running_sum = jnp.sum(weights, axis=2) + fresh_weight
    weighted = jnp.einsum(
        "shk,skd->shd",
        weights.astype(jnp.bfloat16),
        gathered_values,
        preferred_element_type=jnp.float32,
    )
    weighted = weighted + fresh_weight.astype(jnp.bfloat16).astype(jnp.float32)[
        ..., None
    ] * newest_entry[:, None, head_dim:].astype(jnp.float32)
    partial_value = (running_max, running_sum, weighted)
    bit_count = group_size.bit_length() - 1
    for bit_index in reversed(range(bit_count)):
        half_heads = partial_value[0].shape[1] // 2
        keep_half = quarter >> bit_index & 1
        kept = head_slice(partial_value, keep_half * half_heads, half_heads)
        sent = head_slice(partial_value, (1 - keep_half) * half_heads, half_heads)
        partner = from_partner(sent, "head", bit_index)
        partial_value = merge_pair(kept, partner)
    attention = (
        (partial_value[2] / partial_value[1][..., None])
        .reshape(seq_count, block_cols)
        .astype(jnp.bfloat16)
    )
    head_terms = jnp.dot(
        lax.all_gather(attention, "batch", axis=0, tiled=True),
        out_weight,
        preferred_element_type=jnp.float32,
    )
    projected = lax.psum(head_terms, ("sect", "head"))
    hidden_state = residual.astype(jnp.float32) + projected
    squares = lax.psum(jnp.sum(hidden_state * hidden_state, axis=1), "batch")
    inverse = lax.rsqrt(squares / D + NORM_EPS)
    normed = (hidden_state * inverse[:, None] * norm_gain[None, :]).astype(jnp.bfloat16)
    token_count, top_count = expert_ids.shape
    capacity = 2 * token_count * top_count // EXPERTS
    pair_local = gate_up_weight.shape[0]
    flat_ids = expert_ids.reshape(-1)
    one_hot = (flat_ids[:, None] == jnp.arange(EXPERTS, dtype=jnp.int32)[None, :]).astype(jnp.int32)
    earlier = jnp.cumsum(one_hot, axis=0) - one_hot
    rank_in = jnp.sum(earlier * one_hot, axis=1)
    sub_half = lax.axis_index("head") // (head_size // 2)
    pair_first = lax.axis_index("sect") * (batch_size * pair_local)
    local_pair = flat_ids // 2 - pair_first
    in_sect = (local_pair >= 0) & (local_pair < batch_size * pair_local)
    full_slot = (
        (local_pair // pair_local * 2 + flat_ids % 2) * pair_local + local_pair % pair_local
    ) * capacity + rank_in
    full_slot = jnp.where(in_sect, full_slot, -1)
    slot_dev = pair_local * capacity
    slot_total = batch_size * 2 * slot_dev
    send_count = batch_size * slot_dev
    matches = (
        full_slot.reshape(token_count, top_count)[None, :, :]
        == jnp.arange(slot_total, dtype=jnp.int32)[:, None, None]
    )
    selector_full = (
        jnp.any(matches, axis=2).astype(jnp.bfloat16).reshape(batch_size, 2, slot_dev, token_count)
    )
    selector = lax.dynamic_index_in_dim(selector_full, sub_half, 1, keepdims=False).reshape(
        send_count, token_count
    )
    coefficient = route_weight / jnp.sum(route_weight, axis=1, keepdims=True)
    combine_full = jnp.sum(jnp.where(matches, coefficient[None, :, :], 0.0), axis=2).T
    cols_dev = normed.shape[1]
    outgoing = jnp.dot(selector, normed, preferred_element_type=jnp.float32).astype(jnp.bfloat16)
    outgoing = outgoing.reshape(batch_size, pair_local, capacity, cols_dev)
    arrived = lax.all_to_all(outgoing, "batch", split_axis=0, concat_axis=3, tiled=True)[0]
    mixture = jnp.einsum(
        "ecd,edgf->ecgf", arrived, gate_up_weight, preferred_element_type=jnp.float32
    )
    activated = (jax.nn.silu(mixture[:, :, 0]) * mixture[:, :, 1]).astype(jnp.bfloat16)
    expert_part = jnp.einsum(
        "ecf,efd->ecd", activated, down_weight, preferred_element_type=jnp.float32
    )
    leaving = expert_part.reshape(1, slot_dev, batch_size, cols_dev)
    came_back = (
        lax.all_to_all(
            leaving.astype(jnp.bfloat16), "batch", split_axis=2, concat_axis=0, tiled=True
        )
        .astype(leaving.dtype)
        .reshape(send_count, cols_dev)
    )
    weights_used = lax.dynamic_index_in_dim(
        combine_full.reshape(token_count, batch_size, 2, slot_dev), sub_half, 2, keepdims=False
    )
    weights_used = weights_used.reshape(token_count, send_count)
    combined = jnp.dot(weights_used, came_back, preferred_element_type=jnp.float32)
    expert_mix = lax.psum(combined, ("sect", "head"))
    return (hidden_state + expert_mix).astype(jnp.bfloat16)


def solution(mesh):
    placed = (
        P("batch", "head", "sect"),
        P("batch", None, None),
        P("batch", ("sect", "head"), None, None),
        P("batch"),
        P("batch", None, None),
        P(("sect", "head"), "batch"),
        P(None, "batch"),
        P("batch"),
        P(),
        P(),
        P(("sect", "batch"), None, None, "head"),
        P(("sect", "batch"), "head", None),
    )
    return jax.shard_map(
        on_device, mesh=mesh, in_specs=placed, out_specs=P(None, "batch"), check_vma=False
    )
```

profile of v0, /device:TPU:32, one launch (start us, length us, event | category | flops | bytes accessed | tf_op | source)
XLA Modules:
  0.0 342.4 jit_solution(5951458100370429770)
XLA Ops:
  6.5 0.7 copy.66
  7.3 34.3 %all_gather.6 = bf16[6,16,256]{2,0,1:T(8,128)(2,1)S(1)} all-gather(bf16[6,2,256]{2,0,1:T(8,128)(2,1)S(1)} %copy.66), channel_id=1, replica_groups=mesh['sect'=2,'batch'=16,'head'=8] {'head'}, dimensions={1}, use_global_device_ids=true | all-gather | bytes 55296 | tf_op jit(solution)/shard_map/all_gather | solution.py:87
  41.6 0.7 constant_dynamic-slice_fusion.14
  42.3 0.2 compare_reduce_fusion
  42.5 0.1 and.72
  42.6 0.1 and.73
  42.9 3.2 fusion.49
  46.2 0.1 fusion.29
  46.4 1.3 fusion.50
  47.8 1.2 fusion.8
  49.1 2.0 collective-permute-start.4
  51.1 1.4 convolution_add_fusion
  52.5 0.1 collective-permute-start.1
  52.7 0.1 copy.69
  52.7 0.1 eq.65
  53.0 1.8 reduce-window.6
  54.8 0.3 slice_reduce_fusion
  55.1 0.1 fusion.13
  55.4 0.8 fusion.2
  56.2 0.2 copy.78
  56.6 3.2 collective-permute-start.2
  59.9 0.3 collective-permute-start.5
  60.3 3.3 collective-permute-start.3
  63.6 1.4 collective-permute-done.5
  65.0 0.5 collective-permute-done.3
  65.7 18.2 %all-gather = bf16[16,6,512]{2,1,0:T(8,128)(2,1)S(1)} all-gather(bf16[1,6,512]{2,1,0:T(8,128)(2,1)S(1)} %reshape.182), channel_id=1, replica_groups=mesh['sect'=2,'batch'=16,'head'=8] {'batch'}, dimensions={0}, use_global_device_ids=true | all-gather | bytes 104448 | tf_op jit(solution)/shard_map/all_gather | solution.py:152
  83.9 0.8 fusion.51
  84.8 94.1 %all-reduce.3.cloned.1.call-done = f32[96,256]{1,0:T(8,128)} async-done(((f32[96,256]{1,0:T(8,128)}), f32[96,256]{1,0:T(8,128)}) %all-reduce.3.cloned.1.call-update) | async-done | bytes 98320 | tf_op jit(solution)/shard_map/psum | solution.py:156
  178.9 1.0 multiply_reduce_fusion
  180.0 21.5 %psum.22 = f32[96]{0:T(128)S(1)} all-reduce(f32[96]{0:T(128)S(1)} %multiply_reduce_fusion), channel_id=1, replica_groups=mesh['sect'=2,'batch'=16,'head'=8] {'batch'}, use_global_device_ids=true, to_apply=%region_11.12 | all-reduce | flops 96 | bytes 768 | tf_op jit(solution)/shard_map/psum | solution.py:158
  201.4 1.8 convolution_convert_fusion.1
  203.3 9.6 %all-to-all-start = ((bf16[16,1,24,256]{3,2,1,0:T(8,128)(2,1)}), bf16[16,1,24,256]{3,2,1,0:T(8,128)(2,1)}, u32[]{:S(2)}, u32[]{:S(2)}) async-start(bf16[16,1,24,256]{3,2,1,0:T(8,128)(2,1)} %bitcast.13), calls=%async_computation | async-start | bytes 393216 | tf_op jit(solution)/shard_map/all_to_all | solution.py:194
  212.9 3.4 %copy.86 = bf16[4096,384]{1,0:T(8,128)(2,1)S(1)} copy(bf16[4096,384]{0,1:T(8,128)(2,1)} %bitcast.92) | data formatting | bytes 6291456 | tf_op jit(solution)/shard_map/ecf,efd->ecd/dot_general | solution.py:199
  216.3 0.6 reduce_sum.50
  216.9 4.6 %all-to-all-done = bf16[16,1,24,256]{3,2,1,0:T(8,128)(2,1)} async-done(((bf16[16,1,24,256]{3,2,1,0:T(8,128)(2,1)}), bf16[16,1,24,256]{3,2,1,0:T(8,128)(2,1)}, u32[]{:S(2)}, u32[]{:S(2)}) %all-to-all-start) | async-done | bytes 196640 | tf_op jit(solution)/shard_map/all_to_all | solution.py:194
  221.5 1.6 copy.80
  223.1 1.7 reshape.187
  224.8 3.8 %fusion.5 = f32[1,24,2,384]{3,1,2,0:T(8,128)S(1)} fusion(bf16[24,4096,1]{1,0,2:T(8,128)(2,1)} %reshape.187, bf16[4096,2,384]{2,1,0:T(2,128)(2,1)} %bitcast.102), kind=kOutput, calls=%fused_computation.10 | convolution fusion | flops 150994944 | bytes 6561792 | tf_op jit(solution)/shard_map/ecd,edgf->ecgf/dot_general | solution.py:195
  228.7 1.9 fusion.4
  230.6 4.8 %all-to-all-start.1 = ((bf16[1,24,16,256]{3,1,0,2:T(8,128)(2,1)}), bf16[1,24,16,256]{3,1,0,2:T(8,128)(2,1)S(1)}, u32[]{:S(2)}, u32[]{:S(2)}) async-start(bf16[1,24,16,256]{3,1,0,2:T(8,128)(2,1)} %fusion.4), calls=%async_computation.1 | async-start | bytes 393216 | tf_op jit(solution)/shard_map/all_to_all | solution.py:204
  235.4 0.7 broadcast_divide_fusion
  236.1 0.1 copy.76
  236.2 1.6 select_reduce_fusion
  237.8 0.2 copy.77
  238.0 5.8 %all-to-all-done.1 = bf16[1,24,16,256]{3,1,0,2:T(8,128)(2,1)S(1)} async-done(((bf16[1,24,16,256]{3,1,0,2:T(8,128)(2,1)}), bf16[1,24,16,256]{3,1,0,2:T(8,128)(2,1)S(1)}, u32[]{:S(2)}, u32[]{:S(2)}) %all-to-all-start.1) | async-done | bytes 196640 | tf_op jit(solution)/shard_map/all_to_all | solution.py:204
  243.8 0.8 fusion.52
  244.7 89.4 %all-reduce.5.cloned.1.call-done = f32[96,256]{1,0:T(8,128)} async-done(((f32[96,256]{1,0:T(8,128)}), f32[96,256]{1,0:T(8,128)}) %all-reduce.5.cloned.1.call-update) | async-done | bytes 98320 | tf_op jit(solution)/shard_map/psum | solution.py:215
  334.0 1.5 add_convert_fusion
  (58 shorter events, 1.4 us)
Async XLA Ops:
  6.5 77.4 %copy-start = (bf16[512,256]{1,0:T(8,128)(2,1)S(1)}, bf16[512,256]{1,0:T(8,128)(2,1)}, u32[]{:S(2)}) copy-start(bf16[512,256]{1,0:T(8,128)(2,1)} %param.17) | copy-start | bytes 786436
  6.5 172.4 %all-reduce.3.cloned.1.call-start = ((), (), s32[]{:S(2)}) async-start(), calls=%async_computation.2 | async-start | bytes 196608 | tf_op jit(solution)/shard_map/psum | solution.py:156
  42.9 3.2 copy-start.6
  42.9 3.4 %copy-start.8 = (s32[6]{0:T(128)S(1)}, s32[6]{0:T(128)}, u32[]{:S(2)}) copy-start(s32[6]{0:T(128)} %param.15) | copy-start | bytes 76
  46.2 6.5 %copy-start.5 = (s32[96,8]{0,1:T(8,128)S(1)}, s32[96,8]{0,1:T(8,128)}, u32[]{:S(2)}) copy-start(s32[96,8]{0,1:T(8,128)} %param.20) | copy-start | bytes 9220
  47.7 8.7 %collective-permute-start = (f32[6,8]{1,0:T(8,128)S(1)}, f32[6,8]{1,0:T(8,128)S(1)}, u32[]{:S(2)}, u32[]{:S(2)}) collective-permute-start(f32[6,8]{1,0:T(8,128)S(1)} %constant_dynamic-slice_fusion.10), channel_id=1, source_target_pairs={{0,2},{1,3},{2,0},{3,1},{4,6},{5,7},{6,4},{7,5},{8,10},{9,11},{10,... | collective-permute-start | bytes 584 | tf_op jit(solution)/shard_map/ppermute | solution.py:30
  49.1 7.3 %collective-permute-start.4 = (f32[6,8]{1,0:T(8,128)S(1)}, f32[6,8]{1,0:T(8,128)S(1)}, u32[]{:S(2)}, u32[]{:S(2)}) collective-permute-start(f32[6,8]{1,0:T(8,128)S(1)} %constant_dynamic-slice_fusion.4), channel_id=1, source_target_pairs={{0,2},{1,3},{2,0},{3,1},{4,6},{5,7},{6,4},{7,5},{8,10},{9,11},{10,... | collective-permute-start | bytes 584 | tf_op jit(solution)/shard_map/ppermute | solution.py:30
  51.1 127.8 %copy-start.2 = (bf16[96,256]{1,0:T(8,128)(2,1)S(1)}, bf16[96,256]{1,0:T(8,128)(2,1)}, u32[]{:S(2)}) copy-start(bf16[96,256]{1,0:T(8,128)(2,1)} %param.18) | copy-start | bytes 147460
  51.1 150.3 %copy-start.7 = (f32[256]{0:T(256)S(1)}, f32[256]{0:T(256)}, u32[]{:S(2)}) copy-start(f32[256]{0:T(256)} %param.19) | copy-start | bytes 3076
  52.5 7.7 %collective-permute-start.1 = (f32[6,8,128]{2,1,0:T(8,128)S(1)}, f32[6,8,128]{2,1,0:T(8,128)S(1)}, u32[]{:S(2)}, u32[]{:S(2)}) collective-permute-start(f32[6,8,128]{2,1,0:T(8,128)S(1)} %constant_dynamic-slice_fusion.9), channel_id=1, source_target_pairs={{0,2},{1,3},{2,0},{3,1},{4,6},{5,7},{6,4},{7,5},{8,10},{9,11},{10,... | collective-permute-start | bytes 73736 | tf_op jit(solution)/shard_map/ppermute | solution.py:30
  55.4 157.5 %copy-start.3 = (s32[96,8]{1,0:T(8,128)}, s32[96,8]{1,0:T(8,128)S(1)}, u32[]{:S(2)}) copy-start(s32[96,8]{1,0:T(8,128)S(1)} %fusion.22) | copy-start | bytes 9220
  56.6 7.0 %collective-permute-start.2 = (f32[6,4]{1,0:T(8,128)S(1)}, f32[6,4]{1,0:T(8,128)S(1)}, u32[]{:S(2)}, u32[]{:S(2)}) collective-permute-start(f32[6,4]{1,0:T(8,128)S(1)} %constant_dynamic-slice_fusion.7), channel_id=1, source_target_pairs={{0,1},{1,0},{2,3},{3,2},{4,5},{5,4},{6,7},{7,6},{8,9},{9,8},{10,11... | collective-permute-start | bytes 296 | tf_op jit(solution)/shard_map/ppermute | solution.py:30
  59.9 5.1 %collective-permute-start.5 = (f32[6,4]{1,0:T(8,128)S(1)}, f32[6,4]{1,0:T(8,128)S(1)}, u32[]{:S(2)}, u32[]{:S(2)}) collective-permute-start(f32[6,4]{1,0:T(8,128)S(1)} %constant_dynamic-slice_fusion.2), channel_id=1, source_target_pairs={{0,1},{1,0},{2,3},{3,2},{4,5},{5,4},{6,7},{7,6},{8,9},{9,8},{10,11... | collective-permute-start | bytes 296 | tf_op jit(solution)/shard_map/ppermute | solution.py:30
  60.3 5.3 %collective-permute-start.3 = (f32[6,4,128]{2,1,0:T(4,128)S(1)}, f32[6,4,128]{2,1,0:T(4,128)S(1)}, u32[]{:S(2)}, u32[]{:S(2)}) collective-permute-start(f32[6,4,128]{2,1,0:T(4,128)S(1)} %constant_dynamic-slice_fusion.6), channel_id=1, source_target_pairs={{0,1},{1,0},{2,3},{3,2},{4,5},{5,4},{6,7},{7,6},{8,9},{9,8},{10,11... | collective-permute-start | bytes 36872 | tf_op jit(solution)/shard_map/ppermute | solution.py:30
  203.3 18.2 %all-to-all-start = ((bf16[16,1,24,256]{3,2,1,0:T(8,128)(2,1)}), bf16[16,1,24,256]{3,2,1,0:T(8,128)(2,1)}, u32[]{:S(2)}, u32[]{:S(2)}) async-start(bf16[16,1,24,256]{3,2,1,0:T(8,128)(2,1)} %bitcast.13), calls=%async_computation | async-start | bytes 393216 | tf_op jit(solution)/shard_map/all_to_all | solution.py:194
  212.9 3.4 %copy-start.4 = (f32[96,8]{0,1:T(8,128)S(1)}, f32[96,8]{0,1:T(8,128)}, u32[]{:S(2)}) copy-start(f32[96,8]{0,1:T(8,128)} %param.21) | copy-start | bytes 9220
  228.7 105.4 %copy-start.1 = (f32[96,256]{1,0:T(8,128)S(1)}, f32[96,256]{1,0:T(8,128)}, u32[]{:S(2)}) copy-start(f32[96,256]{1,0:T(8,128)} %all-reduce.3.cloned.1.call-done) | copy-start | bytes 294916
  230.6 13.3 %all-to-all-start.1 = ((bf16[1,24,16,256]{3,1,0,2:T(8,128)(2,1)}), bf16[1,24,16,256]{3,1,0,2:T(8,128)(2,1)S(1)}, u32[]{:S(2)}, u32[]{:S(2)}) async-start(bf16[1,24,16,256]{3,1,0,2:T(8,128)(2,1)} %fusion.4), calls=%async_computation.1 | async-start | bytes 393216 | tf_op jit(solution)/shard_map/all_to_all | solution.py:204
  235.3 98.7 %all-reduce.5.cloned.1.call-start = ((), (), s32[]{:S(2)}) async-start(), calls=%async_computation.3 | async-start | bytes 196608 | tf_op jit(solution)/shard_map/psum | solution.py:215
Sparse Core Ops, SparseCore 0:
  84.9 94.0 all-reduce.2
  244.8 89.1 all-reduce.4
where the time goes:
time: 343 us; the launch traced here: 342 us
  waiting for transfers between devices  196 us (57%)
  blocking collectives  73.9 us (22%)
  starting transfers between devices  23.4 us (7%)
  between operations  13.7 us (4%)
  local copies, waits for them, and re-layouts  13.3 us (4%)
  matrix products  12 us (3%)
  other arithmetic  10.2 us (3%)
    psum x1, waiting for transfers between devices, on_device(): projected = lax.psum(head_terms, ('sect', 'head'))  94.1 us
    psum x1, waiting for transfers between devices, on_device(): expert_mix = lax.psum(combined, ('sect', 'head'))  89.4 us
    all_gather x1, blocking collectives, on_device(): all_heads = lax.all_gather(queries, 'head', axis=1, tiled=True)  34.3 us
    psum x1, blocking collectives, on_device(): squares = lax.psum(jnp.sum(hidden_state * hidden_state, axis=1), 'batch')  21.5 us
    all_gather x1, blocking collectives, on_device(): lax.all_gather(attention, 'batch', axis=0, tiled=True)  18.2 us
    all_to_all x1, starting transfers between devices, on_device(): lax.all_to_all(outgoing, 'batch', split_axis=0, concat_axis=3, tiled=True)  9.58 us
    ppermute x6, starting transfers between devices, from_partner(): lax.ppermute(shard, axis, [(i, i ^ 1 << distance) for i in range(lax.axis...  9.03 us
  transfers between devices with their start and end apart: 10, of which 6 were waited for; matrix products, arithmetic and copies ran while one was open for 4% of the time, Pallas kernels for 0%

commit v1 on v0

--- a/solution.py
+++ b/solution.py
@@ -8,6 +8,19 @@
 EXPERTS = 64
 NEG_FILL = -1e30
 NORM_EPS = 1e-06
+
+
+def collect(x, axis, dim):
+    ways = lax.axis_size(axis)
+    up = [(d, (d + 1) % ways) for d in range(ways)]
+    down = [(d, (d - 1) % ways) for d in range(ways)]
+    earlier, later = ([x], [x])
+    for _ in range(ways // 2):
+        earlier.append(lax.ppermute(earlier[-1], axis, up))
+    for _ in range((ways - 1) // 2):
+        later.append(lax.ppermute(later[-1], axis, down))
+    line = jnp.concatenate([*earlier[::-1], *later[1:]], axis=dim)
+    return jnp.roll(line, (lax.axis_index(axis) - ways // 2) * x.shape[dim], axis=dim)
 
 
 def copy_for_each(shard, axis):
@@ -149,9 +162,7 @@
         .astype(jnp.bfloat16)
     )
     head_terms = jnp.dot(
-        lax.all_gather(attention, "batch", axis=0, tiled=True),
-        out_weight,
-        preferred_element_type=jnp.float32,
+        collect(attention, "batch", 0), out_weight, preferred_element_type=jnp.float32
     )
     projected = lax.psum(head_terms, ("sect", "head"))
     hidden_state = residual.astype(jnp.float32) + projected

time: 343 us -> 362 us (1.055)
  waiting for transfers between devices: 196 us -> 216 us
  blocking collectives: 73.9 us -> 55.7 us
  starting transfers between devices: 23.4 us -> 39.6 us
    all_gather x1 -> x0, blocking collectives: 18.2 us -> none  [on_device(): lax.all_gather(attention, 'batch', axis=0, tiled=True)]
    ppermute x0 -> x15, starting transfers between devices: none -> 16.3 us  [the longest x7 16 us: collect(): later.append(lax.ppermute(later[-1], axis, down))]
    ppermute x0 -> x15, waiting for transfers between devices: none -> 10.7 us  [the longest x8 8.51 us: collect(): earlier.append(lax.ppermute(earlier[-1], axis, up))]
    psum x1, waiting for transfers between devices: 94.1 us -> 99.5 us  [on_device(): projected = lax.psum(head_terms, ('sect', 'head'))]
  transfers between devices with their start and end apart: 10 -> 25, of which waited for: 6 -> 18; matrix products, arithmetic and copies ran while one was open for 4% -> 3% of each run, Pallas kernels for 0% -> 0%
where the time goes in v1:
time: 362 us; the launch traced here: 361 us
  waiting for transfers between devices  216 us (60%)
  blocking collectives  55.7 us (15%)
  starting transfers between devices  39.6 us (11%)
  local copies, waits for them, and re-layouts  15.8 us (4%)
  between operations  13.8 us (4%)
  matrix products  11.4 us (3%)
  other arithmetic  9.2 us (3%)
    psum x1, waiting for transfers between devices, on_device(): projected = lax.psum(head_terms, ('sect', 'head'))  99.5 us
    psum x1, waiting for transfers between devices, on_device(): expert_mix = lax.psum(combined, ('sect', 'head'))  89.4 us
    all_gather x1, blocking collectives, on_device(): all_heads = lax.all_gather(queries, 'head', axis=1, tiled=True)  34.3 us
    psum x1, blocking collectives, on_device(): squares = lax.psum(jnp.sum(hidden_state * hidden_state, axis=1), 'batch')  21.5 us
    ppermute x7, starting transfers between devices, collect(): later.append(lax.ppermute(later[-1], axis, down))  16 us
    all_to_all x1, starting transfers between devices, on_device(): lax.all_to_all(outgoing, 'batch', split_axis=0, concat_axis=3, tiled=True)  9.58 us
    ppermute x6, starting transfers between devices, from_partner(): lax.ppermute(shard, axis, [(i, i ^ 1 << distance) for i in range(lax.axis...  8.98 us
    ppermute x8, waiting for transfers between devices, collect(): earlier.append(lax.ppermute(earlier[-1], axis, up))  8.51 us
  transfers between devices with their start and end apart: 25, of which 18 were waited for; matrix products, arithmetic and copies ran while one was open for 3% of the time, Pallas kernels for 0%

profile of v1, /device:TPU:32, one launch (start us, length us, event | category | flops | bytes accessed | tf_op | source)
XLA Modules:
  0.0 361.1 jit_solution(3102356886861746756)
XLA Ops:
  6.5 0.7 copy.66
  7.3 34.3 %all_gather.3 = bf16[6,16,256]{2,0,1:T(8,128)(2,1)S(1)} all-gather(bf16[6,2,256]{2,0,1:T(8,128)(2,1)S(1)} %copy.66), channel_id=1, replica_groups=mesh['sect'=2,'batch'=16,'head'=8] {'head'}, dimensions={1}, use_global_device_ids=true | all-gather | bytes 55296 | tf_op jit(solution)/shard_map/all_gather | solution.py:100
  41.6 0.7 constant_dynamic-slice_fusion.14
  42.9 3.2 fusion.53
  47.0 0.7 copy-done.1
  48.0 1.4 convolution_add_fusion
  49.6 2.0 collective-permute-start
  51.7 1.7 collective-permute-done
  53.4 1.9 collective-permute-done.4
  55.4 3.2 collective-permute-start.2
  59.2 3.3 collective-permute-start.3
  62.4 1.4 collective-permute-done.5
  64.6 1.7 collective-permute-start.14
  66.3 1.3 collective-permute-done.6
  67.7 1.7 collective-permute-start.15
  69.4 1.3 collective-permute-done.7
  70.9 1.8 collective-permute-start.16
  72.7 1.1 collective-permute-done.8
  73.8 1.8 reduce-window.6
  75.6 1.9 collective-permute-start.17
  78.1 0.8 collective-permute-done.17
  78.9 3.1 collective-permute-start.18
  82.7 0.6 collective-permute-done.18
  83.3 3.0 collective-permute-start.19
  86.8 0.8 collective-permute-done.19
  87.6 2.9 collective-permute-start.20
  91.1 0.8 fusion.2
  92.1 3.2 collective-permute-done.13
  95.3 1.9 concatenate.6
  97.2 0.8 fusion.18
  98.1 99.5 %all-reduce.3.cloned.1.call-done = f32[96,256]{1,0:T(8,128)} async-done(((f32[96,256]{1,0:T(8,128)}), f32[96,256]{1,0:T(8,128)}) %all-reduce.3.cloned.1.call-update) | async-done | bytes 98320 | tf_op jit(solution)/shard_map/psum | solution.py:167
  197.6 1.0 multiply_reduce_fusion
  198.6 21.5 %psum.22 = f32[96]{0:T(128)S(1)} all-reduce(f32[96]{0:T(128)S(1)} %multiply_reduce_fusion), channel_id=1, replica_groups=mesh['sect'=2,'batch'=16,'head'=8] {'batch'}, use_global_device_ids=true, to_apply=%region_11.12 | all-reduce | flops 96 | bytes 768 | tf_op jit(solution)/shard_map/psum | solution.py:169
  220.1 1.9 convolution_convert_fusion.1
  221.9 9.6 %all-to-all-start = ((bf16[16,1,24,256]{3,2,1,0:T(8,128)(2,1)}), bf16[16,1,24,256]{3,2,1,0:T(8,128)(2,1)}, u32[]{:S(2)}, u32[]{:S(2)}) async-start(bf16[16,1,24,256]{3,2,1,0:T(8,128)(2,1)} %bitcast.13), calls=%async_computation | async-start | bytes 393216 | tf_op jit(solution)/shard_map/all_to_all | solution.py:205
  231.5 3.4 copy.86
  235.6 4.6 %all-to-all-done = bf16[16,1,24,256]{3,2,1,0:T(8,128)(2,1)} async-done(((bf16[16,1,24,256]{3,2,1,0:T(8,128)(2,1)}), bf16[16,1,24,256]{3,2,1,0:T(8,128)(2,1)}, u32[]{:S(2)}, u32[]{:S(2)}) %all-to-all-start) | async-done | bytes 196640 | tf_op jit(solution)/shard_map/all_to_all | solution.py:205
  240.2 1.6 copy.80
  241.8 1.7 reshape.184
  243.5 3.8 %fusion.5 = f32[1,24,2,384]{3,1,2,0:T(8,128)S(1)} fusion(bf16[24,4096,1]{1,0,2:T(8,128)(2,1)} %reshape.184, bf16[4096,2,384]{2,1,0:T(2,128)(2,1)} %bitcast.110), kind=kOutput, calls=%fused_computation.10 | convolution fusion | flops 150994944 | bytes 6561792 | tf_op jit(solution)/shard_map/ecd,edgf->ecgf/dot_general | solution.py:206
  247.3 1.9 fusion.4
  249.2 4.8 %all-to-all-start.1 = ((bf16[1,24,16,256]{3,1,0,2:T(8,128)(2,1)}), bf16[1,24,16,256]{3,1,0,2:T(8,128)(2,1)S(1)}, u32[]{:S(2)}, u32[]{:S(2)}) async-start(bf16[1,24,16,256]{3,1,0,2:T(8,128)(2,1)} %fusion.4), calls=%async_computation.1 | async-start | bytes 393216 | tf_op jit(solution)/shard_map/all_to_all | solution.py:215
  254.0 0.7 broadcast_divide_fusion
  254.8 1.6 select_reduce_fusion
  256.6 5.8 %all-to-all-done.1 = bf16[1,24,16,256]{3,1,0,2:T(8,128)(2,1)S(1)} async-done(((bf16[1,24,16,256]{3,1,0,2:T(8,128)(2,1)}), bf16[1,24,16,256]{3,1,0,2:T(8,128)(2,1)S(1)}, u32[]{:S(2)}, u32[]{:S(2)}) %all-to-all-start.1) | async-done | bytes 196640 | tf_op jit(solution)/shard_map/all_to_all | solution.py:215
  262.5 0.8 fusion.55
  263.4 89.4 %all-reduce.5.cloned.1.call-done = f32[96,256]{1,0:T(8,128)} async-done(((f32[96,256]{1,0:T(8,128)}), f32[96,256]{1,0:T(8,128)}) %all-reduce.5.cloned.1.call-update) | async-done | bytes 98320 | tf_op jit(solution)/shard_map/psum | solution.py:226
  352.7 1.5 add_convert_fusion
  (89 shorter events, 7.2 us)
Async XLA Ops:
  6.5 90.7 %copy-start = (bf16[512,256]{1,0:T(8,128)(2,1)S(1)}, bf16[512,256]{1,0:T(8,128)(2,1)}, u32[]{:S(2)}) copy-start(bf16[512,256]{1,0:T(8,128)(2,1)} %param.17) | copy-start | bytes 786436
  6.5 191.1 %all-reduce.3.cloned.1.call-start = ((), (), s32[]{:S(2)}) async-start(), calls=%async_computation.2 | async-start | bytes 196608 | tf_op jit(solution)/shard_map/psum | solution.py:167
  42.9 3.2 copy-start.7
  42.9 3.4 copy-start.9
  47.0 0.8 copy-start.1
  47.0 23.7 %copy-start.6 = (s32[96,8]{0,1:T(8,128)S(1)}, s32[96,8]{0,1:T(8,128)}, u32[]{:S(2)}) copy-start(s32[96,8]{0,1:T(8,128)} %param.20) | copy-start | bytes 9220
  48.0 149.6 %copy-start.3 = (bf16[96,256]{1,0:T(8,128)(2,1)S(1)}, bf16[96,256]{1,0:T(8,128)(2,1)}, u32[]{:S(2)}) copy-start(bf16[96,256]{1,0:T(8,128)(2,1)} %param.18) | copy-start | bytes 147460
  48.0 172.1 %copy-start.8 = (f32[256]{0:T(256)S(1)}, f32[256]{0:T(256)}, u32[]{:S(2)}) copy-start(f32[256]{0:T(256)} %param.19) | copy-start | bytes 3076
  49.4 9.6 %collective-permute-start.1 = (f32[6,8,128]{2,1,0:T(8,128)S(1)}, f32[6,8,128]{2,1,0:T(8,128)S(1)}, u32[]{:S(2)}, u32[]{:S(2)}) collective-permute-start(f32[6,8,128]{2,1,0:T(8,128)S(1)} %constant_dynamic-slice_fusion.9), channel_id=1, source_target_pairs={{0,2},{1,3},{2,0},{3,1},{4,6},{5,7},{6,4},{7,5},{8,10},{9,11},{10,... | collective-permute-start | bytes 73736 | tf_op jit(solution)/shard_map/ppermute | solution.py:43
  49.6 3.8 %collective-permute-start = (f32[6,8]{1,0:T(8,128)S(1)}, f32[6,8]{1,0:T(8,128)S(1)}, u32[]{:S(2)}, u32[]{:S(2)}) collective-permute-start(f32[6,8]{1,0:T(8,128)S(1)} %constant_dynamic-slice_fusion.10), channel_id=1, source_target_pairs={{0,2},{1,3},{2,0},{3,1},{4,6},{5,7},{6,4},{7,5},{8,10},{9,11},{10,... | collective-permute-start | bytes 584 | tf_op jit(solution)/shard_map/ppermute | solution.py:43
  51.7 3.6 collective-permute-start.4
  55.4 7.0 %collective-permute-start.2 = (f32[6,4]{1,0:T(8,128)S(1)}, f32[6,4]{1,0:T(8,128)S(1)}, u32[]{:S(2)}, u32[]{:S(2)}) collective-permute-start(f32[6,4]{1,0:T(8,128)S(1)} %constant_dynamic-slice_fusion.7), channel_id=1, source_target_pairs={{0,1},{1,0},{2,3},{3,2},{4,5},{5,4},{6,7},{7,6},{8,9},{9,8},{10,11... | collective-permute-start | bytes 296 | tf_op jit(solution)/shard_map/ppermute | solution.py:43
  58.7 5.1 %collective-permute-start.5 = (f32[6,4]{1,0:T(8,128)S(1)}, f32[6,4]{1,0:T(8,128)S(1)}, u32[]{:S(2)}, u32[]{:S(2)}) collective-permute-start(f32[6,4]{1,0:T(8,128)S(1)} %constant_dynamic-slice_fusion.2), channel_id=1, source_target_pairs={{0,1},{1,0},{2,3},{3,2},{4,5},{5,4},{6,7},{7,6},{8,9},{9,8},{10,11... | collective-permute-start | bytes 296 | tf_op jit(solution)/shard_map/ppermute | solution.py:43
  59.2 5.3 %collective-permute-start.3 = (f32[6,4,128]{2,1,0:T(4,128)S(1)}, f32[6,4,128]{2,1,0:T(4,128)S(1)}, u32[]{:S(2)}, u32[]{:S(2)}) collective-permute-start(f32[6,4,128]{2,1,0:T(4,128)S(1)} %constant_dynamic-slice_fusion.6), channel_id=1, source_target_pairs={{0,1},{1,0},{2,3},{3,2},{4,5},{5,4},{6,7},{7,6},{8,9},{9,8},{10,11... | collective-permute-start | bytes 36872 | tf_op jit(solution)/shard_map/ppermute | solution.py:43
  64.5 3.1 collective-permute-start.6
  64.6 3.1 collective-permute-start.14
  67.6 3.1 collective-permute-start.7
  67.7 3.2 collective-permute-start.15
  70.7 3.1 collective-permute-start.8
  70.9 4.7 %collective-permute-start.16 = (bf16[6,512]{1,0:T(8,128)(2,1)S(1)}, bf16[6,512]{1,0:T(8,128)(2,1)S(1)}, u32[]{:S(2)}, u32[]{:S(2)}) collective-permute-start(bf16[6,512]{1,0:T(8,128)(2,1)S(1)} %collective-permute-done.15), channel_id=1, source_target_pairs={{0,120},{8,0},{16,8},{24,16},{32,24},{40,32},{48,40},{56,48},{64,5... | collective-permute-start | bytes 18440 | tf_op jit(solution)/shard_map/ppermute | solution.py:21
  73.8 3.7 %collective-permute-start.9 = (bf16[6,512]{1,0:T(8,128)(2,1)S(1)}, bf16[6,512]{1,0:T(8,128)(2,1)S(1)}, u32[]{:S(2)}, u32[]{:S(2)}) collective-permute-start(bf16[6,512]{1,0:T(8,128)(2,1)S(1)} %collective-permute-done.8), channel_id=1, source_target_pairs={{0,8},{8,16},{16,24},{24,32},{32,40},{40,48},{48,56},{56,64},{64,7... | collective-permute-start | bytes 18440 | tf_op jit(solution)/shard_map/ppermute | solution.py:19
  75.6 3.2 collective-permute-start.17
  77.5 5.0 %collective-permute-start.10 = (bf16[6,512]{1,0:T(8,128)(2,1)S(1)}, bf16[6,512]{1,0:T(8,128)(2,1)S(1)}, u32[]{:S(2)}, u32[]{:S(2)}) collective-permute-start(bf16[6,512]{1,0:T(8,128)(2,1)S(1)} %collective-permute-done.9), channel_id=1, source_target_pairs={{0,8},{8,16},{16,24},{24,32},{32,40},{40,48},{48,56},{56,64},{64,7... | collective-permute-start | bytes 18440 | tf_op jit(solution)/shard_map/ppermute | solution.py:19
  78.9 4.5 %collective-permute-start.18 = (bf16[6,512]{1,0:T(8,128)(2,1)S(1)}, bf16[6,512]{1,0:T(8,128)(2,1)S(1)}, u32[]{:S(2)}, u32[]{:S(2)}) collective-permute-start(bf16[6,512]{1,0:T(8,128)(2,1)S(1)} %collective-permute-done.17), channel_id=1, source_target_pairs={{0,120},{8,0},{16,8},{24,16},{32,24},{40,32},{48,40},{56,48},{64,5... | collective-permute-start | bytes 18440 | tf_op jit(solution)/shard_map/ppermute | solution.py:21
  82.4 4.3 %collective-permute-start.11 = (bf16[6,512]{1,0:T(8,128)(2,1)S(1)}, bf16[6,512]{1,0:T(8,128)(2,1)S(1)}, u32[]{:S(2)}, u32[]{:S(2)}) collective-permute-start(bf16[6,512]{1,0:T(8,128)(2,1)S(1)} %collective-permute-done.10), channel_id=1, source_target_pairs={{0,8},{8,16},{16,24},{24,32},{32,40},{40,48},{48,56},{56,64},{64,7... | collective-permute-start | bytes 18440 | tf_op jit(solution)/shard_map/ppermute | solution.py:19
  83.3 4.3 %collective-permute-start.19 = (bf16[6,512]{1,0:T(8,128)(2,1)S(1)}, bf16[6,512]{1,0:T(8,128)(2,1)S(1)}, u32[]{:S(2)}, u32[]{:S(2)}) collective-permute-start(bf16[6,512]{1,0:T(8,128)(2,1)S(1)} %collective-permute-done.18), channel_id=1, source_target_pairs={{0,120},{8,0},{16,8},{24,16},{32,24},{40,32},{48,40},{56,48},{64,5... | collective-permute-start | bytes 18440 | tf_op jit(solution)/shard_map/ppermute | solution.py:21
  86.8 4.3 %collective-permute-start.12 = (bf16[6,512]{1,0:T(8,128)(2,1)S(1)}, bf16[6,512]{1,0:T(8,128)(2,1)S(1)}, u32[]{:S(2)}, u32[]{:S(2)}) collective-permute-start(bf16[6,512]{1,0:T(8,128)(2,1)S(1)} %collective-permute-done.11), channel_id=1, source_target_pairs={{0,8},{8,16},{16,24},{24,32},{32,40},{40,48},{48,56},{56,64},{64,7... | collective-permute-start | bytes 18440 | tf_op jit(solution)/shard_map/ppermute | solution.py:19
  86.8 144.7 %copy-start.4 = (s32[96,8]{1,0:T(8,128)}, s32[96,8]{1,0:T(8,128)S(1)}, u32[]{:S(2)}) copy-start(s32[96,8]{1,0:T(8,128)S(1)} %fusion.24) | copy-start | bytes 9220
  87.6 4.5 %collective-permute-start.20 = (bf16[6,512]{1,0:T(8,128)(2,1)S(1)}, bf16[6,512]{1,0:T(8,128)(2,1)S(1)}, u32[]{:S(2)}, u32[]{:S(2)}) collective-permute-start(bf16[6,512]{1,0:T(8,128)(2,1)S(1)} %collective-permute-done.19), channel_id=1, source_target_pairs={{0,120},{8,0},{16,8},{24,16},{32,24},{40,32},{48,40},{56,48},{64,5... | collective-permute-start | bytes 18440 | tf_op jit(solution)/shard_map/ppermute | solution.py:21
  91.1 4.3 %collective-permute-start.13 = (bf16[6,512]{1,0:T(8,128)(2,1)S(1)}, bf16[6,512]{1,0:T(8,128)(2,1)S(1)}, u32[]{:S(2)}, u32[]{:S(2)}) collective-permute-start(bf16[6,512]{1,0:T(8,128)(2,1)S(1)} %collective-permute-done.12), channel_id=1, source_target_pairs={{0,8},{8,16},{16,24},{24,32},{32,40},{40,48},{48,56},{56,64},{64,7... | collective-permute-start | bytes 18440 | tf_op jit(solution)/shard_map/ppermute | solution.py:19
  221.9 18.2 %all-to-all-start = ((bf16[16,1,24,256]{3,2,1,0:T(8,128)(2,1)}), bf16[16,1,24,256]{3,2,1,0:T(8,128)(2,1)}, u32[]{:S(2)}, u32[]{:S(2)}) async-start(bf16[16,1,24,256]{3,2,1,0:T(8,128)(2,1)} %bitcast.13), calls=%async_computation | async-start | bytes 393216 | tf_op jit(solution)/shard_map/all_to_all | solution.py:205
  231.5 3.4 copy-start.5
  247.3 105.4 %copy-start.2 = (f32[96,256]{1,0:T(8,128)S(1)}, f32[96,256]{1,0:T(8,128)}, u32[]{:S(2)}) copy-start(f32[96,256]{1,0:T(8,128)} %all-reduce.3.cloned.1.call-done) | copy-start | bytes 294916
  249.2 13.3 %all-to-all-start.1 = ((bf16[1,24,16,256]{3,1,0,2:T(8,128)(2,1)}), bf16[1,24,16,256]{3,1,0,2:T(8,128)(2,1)S(1)}, u32[]{:S(2)}, u32[]{:S(2)}) async-start(bf16[1,24,16,256]{3,1,0,2:T(8,128)(2,1)} %fusion.4), calls=%async_computation.1 | async-start | bytes 393216 | tf_op jit(solution)/shard_map/all_to_all | solution.py:215
  254.0 98.7 %all-reduce.5.cloned.1.call-start = ((), (), s32[]{:S(2)}) async-start(), calls=%async_computation.3 | async-start | bytes 196608 | tf_op jit(solution)/shard_map/psum | solution.py:226
Sparse Core Ops, SparseCore 0:
  98.2 99.3 all-reduce.2
  263.5 89.1 all-reduce.4
